TPU v7x, 128 devices: a whole 4x4x4 slice. The times are simulated.
128 devices in a mesh: expert: 32 (over y, z, core), dp: 4 (over x).
Axes of the slice: x: 4, y: 4, z: 4, core: 2. Of those that a mesh axis runs over, the one named last changes fastest.
Arguments:
- activations: bfloat16 [2048, 7168], P(('expert', 'dp')), may hold values from -6 to 6
- cotangent: bfloat16 [2048, 7168], P(('expert', 'dp')), may hold values from -6 to 6
- route_ids: int32 [2048, 8], P(('expert', 'dp')), may hold values from 0 to 31, all different within a row; in each aligned block of 16 rows (0 to 15, 16 to 31, ...) at most 5 rows name the same one
- route_weights: float32 [2048, 8], P(('expert', 'dp')), may hold values from 0.05 to 0.6
- gate_weights: bfloat16 [32, 7168, 1024], P('expert', 'dp'), may hold values from -0.0625 to 0.0625
- up_weights: bfloat16 [32, 7168, 1024], P('expert', 'dp'), may hold values from -0.0625 to 0.0625
- down_weights: bfloat16 [32, 1024, 7168], P('expert', None, 'dp'), may hold values from -0.1875 to 0.1875
Outputs:
- grad_input: bfloat16 [2048, 7168], P(('expert', 'dp'))
- grad_gate: bfloat16 [32, 7168, 1024], P('expert', 'dp')
- grad_up: bfloat16 [32, 7168, 1024], P('expert', 'dp')
- grad_down: bfloat16 [32, 1024, 7168], P('expert', None, 'dp')
Inputs may be any that keep to these rules, and one draw needn't show every extreme that they name: `route_ids`: each token names 8 different experts. Among the routes of one device's 16 tokens, no expert is named more than 5 times, a bound that some block reaches.
All inputs are finite; a program needn't handle non-finite values.
Results may differ from a plain program's by a relative error of at most 0.0064.
Values may be sent and summed in bfloat16 or wider, within the bound.
No kernel may reach another device: no remote copies, remote signals or barrier semaphores. Data moves between devices by JAX's collectives and lax.ppermute only.
A program may use at most 128 MiB of HBM per device.

v0:
```python
import jax
import jax.numpy as jnp
from jax import lax
from jax.sharding import PartitionSpec as P


def swiglu_back(gate, upper, upstream):
    sigma = jax.nn.sigmoid(gate)
    silu_gate = gate * sigma
    activated = (silu_gate * upper).astype(jnp.bfloat16)
    grad_pre = (upstream * upper * sigma * (1.0 + gate * (1.0 - sigma))).astype(jnp.bfloat16)
    grad_lin = (upstream * silu_gate).astype(jnp.bfloat16)
    return (grad_pre, grad_lin, activated)


def contract_rows(left, right):
    return lax.dot_general(
        left, right, (((0,), (0,)), ((), ())), preferred_element_type=jnp.float32
    )


def shards(
    activations, cotangent, route_ids, route_weights, gate_weights, up_weights, down_weights
):
    tok_rows, width = activations.shape
    topk = route_ids.shape[1]
    num_dp = lax.axis_size("dp")
    num_exp = lax.axis_size("expert")
    slice_width = gate_weights.shape[1]
    hidden = gate_weights.shape[2]
    capacity = min(tok_rows, 5 * tok_rows * topk // (4 * num_exp))
    buffer_rows = num_exp * num_dp * capacity
    flat_ids = route_ids.reshape(-1)
    expert_iota = jnp.arange(num_exp, dtype=jnp.int32)
    onehot = (flat_ids[:, None] == expert_iota[None, :]).astype(jnp.int32)
    before = jnp.cumsum(onehot, axis=0) - onehot
    slot = jnp.sum(before * onehot, axis=1)
    target = (flat_ids * capacity + slot).reshape(tok_rows, topk)
    slot_iota = jnp.arange(num_exp * capacity, dtype=jnp.int32)
    matches = target[:, :, None] == slot_iota[None, None, :]
    placing = jnp.any(matches, axis=1).astype(jnp.bfloat16)
    slot_weight = jnp.sum(jnp.where(matches, route_weights[:, :, None], 0.0), axis=(0, 1))
    send_act = contract_rows(placing, activations).astype(jnp.bfloat16)
    send_cot = (contract_rows(placing, cotangent) * slot_weight[:, None]).astype(jnp.bfloat16)
    send_act = send_act.reshape(num_exp, capacity, num_dp, slice_width)
    send_cot = send_cot.reshape(num_exp, capacity, num_dp, slice_width)
    send_both = jnp.concatenate([send_act, send_cot], axis=3)
    flat_both = jnp.swapaxes(send_both, 1, 2).reshape(num_exp * num_dp, capacity, 2 * slice_width)
    recv_both = lax.all_to_all(flat_both, ("expert", "dp"), split_axis=0, concat_axis=0, tiled=True)
    recv_both = recv_both.reshape(buffer_rows, 2 * slice_width)
    act_rows = recv_both[:, :slice_width]
    cot_rows = recv_both[:, slice_width:]
    gate_local = gate_weights[0]
    up_local = up_weights[0]
    down_local = down_weights[0]
    gate_part = jnp.dot(act_rows, gate_local, preferred_element_type=jnp.float32)
    up_part = jnp.dot(act_rows, up_local, preferred_element_type=jnp.float32)
    back_part = lax.dot_general(
        cot_rows, down_local, (((1,), (1,)), ((), ())), preferred_element_type=jnp.float32
    )
    summed = lax.psum_scatter(
        jnp.concatenate([gate_part, up_part, back_part], axis=1),
        "dp",
        scatter_dimension=0,
        tiled=True,
    )
    grad_pre, grad_lin, activated = swiglu_back(
        summed[:, :hidden], summed[:, hidden : 2 * hidden], summed[:, 2 * hidden :]
    )
    gathered = lax.all_gather(
        jnp.concatenate([grad_pre, grad_lin, activated], axis=1), "dp", axis=0, tiled=True
    )
    grad_pre = gathered[:, :hidden]
    grad_lin = gathered[:, hidden : 2 * hidden]
    activated = gathered[:, 2 * hidden :]
    rows_back = lax.dot_general(
        grad_pre, gate_local, (((1,), (1,)), ((), ())), preferred_element_type=jnp.float32
    ) + lax.dot_general(
        grad_lin, up_local, (((1,), (1,)), ((), ())), preferred_element_type=jnp.float32
    )
    grad_gate = contract_rows(act_rows, grad_pre).astype(jnp.bfloat16)[None]
    grad_up = contract_rows(act_rows, grad_lin).astype(jnp.bfloat16)[None]
    grad_down = contract_rows(activated, cot_rows).astype(jnp.bfloat16)[None]
    back_rows = rows_back.astype(jnp.bfloat16)
    flat_back = back_rows.reshape(num_exp * num_dp, capacity, slice_width)
    arrived = lax.all_to_all(flat_back, ("expert", "dp"), split_axis=0, concat_axis=0, tiled=True)
    arrived = jnp.swapaxes(arrived.reshape(num_exp, num_dp, capacity, slice_width), 1, 2)
    arrived = arrived.reshape(num_exp * capacity, width)
    grad_input = jnp.dot(placing, arrived, preferred_element_type=jnp.float32).astype(jnp.bfloat16)
    return (grad_input, grad_gate, grad_up, grad_down)


def solution(mesh):
    placed = (
        P(("expert", "dp"), None),
        P(("expert", "dp"), None),
        P(("expert", "dp"), None),
        P(("expert", "dp"), None),
        P("expert", "dp", None),
        P("expert", "dp", None),
        P("expert", None, "dp"),
    )
    return jax.shard_map(
        shards,
        mesh=mesh,
        in_specs=placed,
        out_specs=(
            P(("expert", "dp"), None),
            P("expert", "dp", None),
            P("expert", "dp", None),
            P("expert", None, "dp"),
        ),
        check_vma=False,
    )
```

profile of v0, /device:TPU:1, one launch (start us, length us, event | category | flops | bytes accessed | tf_op | source)
XLA Modules:
  0.0 347.9 jit_solution(13178940153341892583)
XLA Ops:
  9.7 2.2 fusion
  11.9 3.5 reshape.40
  15.4 2.2 convolution_convert_fusion
  17.6 4.6 %reshape.39 = bf16[32,5,4,1792]{3,2,1,0:T(4,128)(2,1)} reshape(bf16[160,7168]{1,0:T(8,128)(2,1)} %convolution_convert_fusion) | data formatting | bytes 4587520 | tf_op jit(solution)/shard_map/reshape | solution.py:45
  22.2 3.7 %maximum_bitcast_fusion = bf16[32,4,5,3584]{3,1,2,0:T(4,128)(2,1)S(1)} fusion(bf16[32,5,4,1792]{3,2,1,0:T(4,128)(2,1)S(1)} %reshape.40, bf16[32,5,4,1792]{3,2,1,0:T(4,128)(2,1)} %reshape.39), kind=kLoop, calls=%fused_computation.5 | loop fusion | flops 9175040 | bytes 9175040 | tf_op jit(solution)/shard_map/transpose | solution.py:48
  25.9 1.7 copy.36
  27.6 98.5 %all_to_all.10 = bf16[128,5,3584]{2,1,0:T(8,128)(2,1)} all-to-all(bf16[128,5,3584]{2,1,0:T(8,128)(2,1)S(1)} %bitcast.36), channel_id=1, replica_groups=mesh['expert'=32,'dp'=4] {'expert','dp'}, dimensions={0} | all-to-all | bytes 9175040 | tf_op jit(solution)/shard_map/all_to_all | solution.py:49
  126.1 8.1 %reshape.42 = bf16[640,3584]{1,0:T(8,128)(2,1)} reshape(bf16[128,5,3584]{2,1,0:T(8,128)(2,1)} %all_to_all.10) | data formatting | bytes 9175040 | tf_op jit(solution)/shard_map/reshape | solution.py:50
  134.2 5.4 %fusion.1 = f32[640,1024]{1,0:T(8,128)S(1)} fusion(bf16[1,1024,1792]{2,1,0:T(8,128)(2,1)} %param.13, bf16[640,3584]{1,0:T(8,128)(2,1)} %reshape.42), kind=kOutput, calls=%fused_computation.10 | convolution fusion | flops 2348810240 | bytes 8585216 | tf_op jit(solution)/shard_map/dot_general | solution.py:58
  139.7 2.5 fusion.5
  142.2 2.5 fusion.9
  144.8 3.4 pad_maximum_fusion
  148.3 72.4 %reduce-scatter.2.cloned.1.call-done = f32[160,3072]{1,0:T(8,128)} async-done(((f32[640,3072]{1,0:T(8,128)}), f32[160,3072]{1,0:T(8,128)}) %reduce-scatter.2.cloned.1.call-update) | async-done | bytes 1966096 | tf_op jit(solution)/shard_map/reduce_scatter | solution.py:61
  220.7 1.9 multiply_convert_fusion.2
  223.7 45.8 %all-gather.2.cloned.1.call-done = bf16[640,3072]{1,0:T(8,128)(2,1)} async-done(((bf16[160,3072]{1,0:T(8,128)(2,1)}), bf16[640,3072]{1,0:T(8,128)(2,1)}) %all-gather.2.cloned.1.call-update) | async-done | bytes 3932176 | tf_op jit(solution)/shard_map/all_gather | solution.py:70
  269.4 5.2 %fusion.3 = f32[640,1792]{1,0:T(8,128)S(1)} fusion(bf16[1,1792,1024]{2,1,0:T(8,128)(2,1)} %param.12, bf16[640,3072]{1,0:T(8,128)(2,1)} %all-gather.2.cloned.1.call-done), kind=kOutput, calls=%fused_computation.12 | convolution fusion | flops 2348810240 | bytes 9568256 | tf_op jit(solution)/shard_map/dot_general | solution.py:78
  274.6 2.6 add_convert_fusion
  277.2 2.7 reshape.43
  279.9 9.2 %all-to-all-start.1 = ((bf16[128,5,1792]{2,1,0:T(8,128)(2,1)}), bf16[128,5,1792]{2,1,0:T(8,128)(2,1)}, u32[]{:S(2)}, u32[]{:S(2)}) async-start(bf16[128,5,1792]{2,1,0:T(8,128)(2,1)} %reshape.43), calls=%async_computation.2 | async-start | bytes 7340032 | tf_op jit(solution)/shard_map/all_to_all | solution.py:86
  289.1 7.1 %fusion.11 = bf16[1,1792,1024]{2,1,0:T(8,128)(2,1)} fusion(bf16[640,3584]{1,0:T(8,128)(2,1)} %reshape.42, bf16[640,3072]{1,0:T(8,128)(2,1)} %all-gather.2.cloned.1.call-done), kind=kOutput, calls=%fused_computation.20 | convolution fusion | flops 2350645248 | bytes 7274496 | tf_op jit(solution)/shard_map/dot_general | solution.py:17
  296.2 4.5 %fusion.12 = bf16[1,1792,1024]{2,1,0:T(8,128)(2,1)} fusion(bf16[640,3584]{1,0:T(8,128)(2,1)S(1)} %bitcast.40, bf16[640,3072]{1,0:T(8,128)(2,1)S(1)} %copy-done.5), kind=kOutput, calls=%fused_computation.21 | convolution fusion | flops 2350645248 | bytes 7274496 | tf_op jit(solution)/shard_map/dot_general | solution.py:17
  300.8 4.5 %fusion.13 = bf16[1,1024,1792]{2,1,0:T(8,128)(2,1)} fusion(bf16[640,3584]{1,0:T(8,128)(2,1)S(1)} %bitcast.40, bf16[640,3072]{1,0:T(8,128)(2,1)S(1)} %copy-done.5), kind=kOutput, calls=%fused_computation.22 | convolution fusion | flops 2350645248 | bytes 7274496 | tf_op jit(solution)/shard_map/dot_general | solution.py:17
  305.3 31.4 %all-to-all-done.1 = bf16[128,5,1792]{2,1,0:T(8,128)(2,1)} async-done(((bf16[128,5,1792]{2,1,0:T(8,128)(2,1)}), bf16[128,5,1792]{2,1,0:T(8,128)(2,1)}, u32[]{:S(2)}, u32[]{:S(2)}) %all-to-all-start.1) | async-done | bytes 2293792 | tf_op jit(solution)/shard_map/all_to_all | solution.py:86
  336.6 3.0 copy.34
  (40 shorter events, 5.0 us)
Async XLA Ops:
  7.2 2.5 copy-start
  7.2 213.5 %reduce-scatter.2.cloned.1.call-start = ((), (), s32[]{:S(2)}) async-start(), calls=%async_computation.3 | async-start | bytes 9830400 | tf_op jit(solution)/shard_map/reduce_scatter | solution.py:61
  8.2 7.2 %copy-start.3 = (bf16[16,7168]{1,0:T(8,128)(2,1)S(1)}, bf16[16,7168]{1,0:T(8,128)(2,1)}, u32[]{:S(2)}) copy-start(bf16[16,7168]{1,0:T(8,128)(2,1)} %param.7) | copy-start | bytes 688132
  134.2 5.4 %copy-start.2 = (bf16[640,3584]{1,0:T(8,128)(2,1)S(1)}, bf16[640,3584]{1,0:T(8,128)(2,1)}, u32[]{:S(2)}) copy-start(bf16[640,3584]{1,0:T(8,128)(2,1)} %reshape.42) | copy-start | bytes 13762564
  134.2 5.5 %copy-start.6 = (bf16[1,1792,1024]{2,1,0:T(8,128)(2,1)S(1)}, bf16[1,1792,1024]{2,1,0:T(8,128)(2,1)}, u32[]{:S(2)}) copy-start(bf16[1,1792,1024]{2,1,0:T(8,128)(2,1)} %param.12) | copy-start | bytes 11010052
  139.7 2.5 copy-start.7
  148.2 121.2 %all-gather.2.cloned.1.call-start = ((), (), s32[]{:S(2)}) async-start(), calls=%async_computation.4 | async-start | bytes 4915200 | tf_op jit(solution)/shard_map/all_gather | solution.py:70
  269.4 5.2 %copy-start.4 = (bf16[640,3072]{1,0:T(8,128)(2,1)S(1)}, bf16[640,3072]{1,0:T(8,128)(2,1)}, u32[]{:S(2)}) copy-start(bf16[640,3072]{1,0:T(8,128)(2,1)} %all-gather.2.cloned.1.call-done) | copy-start | bytes 11796484
  269.4 5.2 %copy-start.8 = (bf16[1,1792,1024]{2,1,0:T(8,128)(2,1)S(1)}, bf16[1,1792,1024]{2,1,0:T(8,128)(2,1)}, u32[]{:S(2)}) copy-start(bf16[1,1792,1024]{2,1,0:T(8,128)(2,1)} %param.11) | copy-start | bytes 11010052
  279.9 16.3 %slice-start = ((s8[4587520]{0:T(1024)(128)(4,1)}), s8[393216]{0:T(1024)(128)(4,1)S(1)}, s32[]{:S(2)}) async-start(s8[4587520]{0:T(1024)(128)(4,1)} %bitcast.39), calls=%async_computation.5 | async-start | bytes 786432
  279.9 56.7 %all-to-all-start.1 = ((bf16[128,5,1792]{2,1,0:T(8,128)(2,1)}), bf16[128,5,1792]{2,1,0:T(8,128)(2,1)}, u32[]{:S(2)}, u32[]{:S(2)}) async-start(bf16[128,5,1792]{2,1,0:T(8,128)(2,1)} %reshape.43), calls=%async_computation.2 | async-start | bytes 7340032 | tf_op jit(solution)/shard_map/all_to_all | solution.py:86
  289.1 7.1 %slice-start.1 = ((s8[4587520]{0:T(1024)(128)(4,1)}), s8[4194304]{0:T(1024)(128)(4,1)S(1)}, s32[]{:S(2)}) async-start(s8[4587520]{0:T(1024)(128)(4,1)} %bitcast.39), calls=%async_computation.6 | async-start | bytes 8388608
  289.1 7.1 %copy-start.5 = (bf16[640,3072]{1,0:T(8,128)(2,1)S(1)}, bf16[640,3072]{1,0:T(8,128)(2,1)}, u32[]{:S(2)}) copy-start(bf16[640,3072]{1,0:T(8,128)(2,1)} %all-gather.2.cloned.1.call-done) | copy-start | bytes 11796484
  336.6 4.5 %copy-start.1 = (bf16[16,7168]{1,0:T(8,128)(2,1)S(1)}, bf16[16,7168]{1,0:T(8,128)(2,1)}, u32[]{:S(2)}) copy-start(bf16[16,7168]{1,0:T(8,128)(2,1)} %param.8) | copy-start | bytes 688132
Sparse Core Ops, SparseCore 0:
  148.3 72.2 reduce-scatter.1
  223.8 45.6 all-gather.1
where the time goes:
time: 349 us; the launch traced here: 348 us
  waiting for transfers between devices  150 us (43%)
  blocking collectives  98.5 us (28%)
  matrix products  39.8 us (11%)
  local copies, waits for them, and re-layouts  25.7 us (7%)
  between operations  14.3 us (4%)
  other arithmetic  10.8 us (3%)
  starting transfers between devices  9.26 us (3%)
    all_to_all x1, blocking collectives, shards(): lax.all_to_all(flat_both, ('expert', 'dp'), split_axis=0, concat_axis=0,...  98.5 us
    reduce_scatter x1, waiting for transfers between devices, shards(): lax.psum_scatter(jnp.concatenate([gate_part, up_part, back_part], axis=1)...  72.4 us
    all_gather x1, waiting for transfers between devices, shards(): lax.all_gather(jnp.concatenate([grad_pre, grad_lin, activated], axis=1),...  45.8 us
    all_to_all x1, waiting for transfers between devices, shards(): lax.all_to_all(flat_back, ('expert', 'dp'), split_axis=0, concat_axis=0,...  31.4 us
    dot_general x5, matrix products, contract_rows(): lax.dot_general(left, right, (((0,), (0,)), ((), ())), preferred_element_...  20.5 us
    all_to_all x1, starting transfers between devices, shards(): lax.all_to_all(flat_back, ('expert', 'dp'), split_axis=0, concat_axis=0,...  9.18 us
    reshape x1, local copies, waits for them, and re-layouts, shards(): recv_both = recv_both.reshape(buffer_rows, 2 * slice_width)  8.11 us
  transfers between devices with their start and end apart: 3, of which 3 were waited for; matrix products, arithmetic and copies ran while one was open for 5% of the time, Pallas kernels for 0%

commit v1 on v0

--- a/solution.py
+++ b/solution.py
@@ -67,9 +67,22 @@
     grad_pre, grad_lin, activated = swiglu_back(
         summed[:, :hidden], summed[:, hidden : 2 * hidden], summed[:, 2 * hidden :]
     )
-    gathered = lax.all_gather(
-        jnp.concatenate([grad_pre, grad_lin, activated], axis=1), "dp", axis=0, tiled=True
+    shard = jnp.concatenate([grad_pre, grad_lin, activated], axis=1)
+    ways, here, turn = (lax.axis_size("dp"), lax.axis_index("dp"), shard.shape[0])
+    shape = [n * ways if d == 0 else n for d, n in enumerate(shard.shape)]
+    full = lax.dynamic_update_slice_in_dim(
+        jnp.zeros(shape, shard.dtype), shard, here * turn, axis=0
     )
+    going_up = going_down = shard
+    for far in range(1, ways // 2 + 1):
+        going_up = lax.ppermute(going_up, "dp", [(d, (d + 1) % ways) for d in range(ways)])
+        full = lax.dynamic_update_slice_in_dim(full, going_up, (here - far) % ways * turn, axis=0)
+        if 2 * far < ways:
+            going_down = lax.ppermute(going_down, "dp", [(d, (d - 1) % ways) for d in range(ways)])
+            full = lax.dynamic_update_slice_in_dim(
+                full, going_down, (here + far) % ways * turn, axis=0
+            )
+    gathered = full
     grad_pre = gathered[:, :hidden]
     grad_lin = gathered[:, hidden : 2 * hidden]
     activated = gathered[:, 2 * hidden :]

time: 349 us -> 354 us (1.014)
  waiting for transfers between devices: 150 us -> 141 us
  local copies, waits for them, and re-layouts: 25.7 us -> 32.8 us
    all_gather x1 -> x0, waiting for transfers between devices: 45.8 us -> none  [shards(): lax.all_gather(jnp.concatenate([grad_pre, grad_lin, activated], axis=1),...]
    ppermute x0 -> x3, waiting for transfers between devices: none -> 40.4 us  [the longest x2 40.4 us: shards(): lax.ppermute(going_up, 'dp', [(d, (d + 1) % ways) for d in range(ways)])]
    dynamic_update_slice x0 -> x3, local copies, waits for them, and re-layouts: none -> 4.69 us  [the longest x1 2.61 us: shards(): lax.dynamic_update_slice_in_dim(full, going_down, (here + far) % ways * t...]
  transfers between devices with their start and end apart: 3 -> 5, of which waited for: 3 -> 4; matrix products, arithmetic and copies ran while one was open for 5% -> 6% of each run, Pallas kernels for 0% -> 0%
where the time goes in v1:
time: 354 us; the launch traced here: 353 us
  waiting for transfers between devices  141 us (40%)
  blocking collectives  98.5 us (28%)
  matrix products  43 us (12%)
  local copies, waits for them, and re-layouts  32.8 us (9%)
  between operations  14.2 us (4%)
  starting transfers between devices  12 us (3%)
  other arithmetic  11 us (3%)
    all_to_all x1, blocking collectives, shards(): lax.all_to_all(flat_both, ('expert', 'dp'), split_axis=0, concat_axis=0,...  98.5 us
    reduce_scatter x1, waiting for transfers between devices, shards(): lax.psum_scatter(jnp.concatenate([gate_part, up_part, back_part], axis=1)...  72.4 us
    ppermute x2, waiting for transfers between devices, shards(): lax.ppermute(going_up, 'dp', [(d, (d + 1) % ways) for d in range(ways)])  40.4 us
    all_to_all x1, waiting for transfers between devices, shards(): lax.all_to_all(flat_back, ('expert', 'dp'), split_axis=0, concat_axis=0,...  28.4 us
    dot_general x5, matrix products, contract_rows(): lax.dot_general(left, right, (((0,), (0,)), ((), ())), preferred_element_...  23.4 us
    all_to_all x1, starting transfers between devices, shards(): lax.all_to_all(flat_back, ('expert', 'dp'), split_axis=0, concat_axis=0,...  9.33 us
    reshape x1, local copies, waits for them, and re-layouts, shards(): recv_both = recv_both.reshape(buffer_rows, 2 * slice_width)  8.11 us
  transfers between devices with their start and end apart: 5, of which 4 were waited for; matrix products, arithmetic and copies ran while one was open for 6% of the time, Pallas kernels for 0%

profile of v1, /device:TPU:1, one launch (start us, length us, event | category | flops | bytes accessed | tf_op | source)
XLA Modules:
  0.0 352.8 jit_solution(16507439965754084810)
XLA Ops:
  11.9 3.5 reshape.40
  17.6 4.6 %reshape.39 = bf16[32,5,4,1792]{3,2,1,0:T(4,128)(2,1)} reshape(bf16[160,7168]{1,0:T(8,128)(2,1)} %convolution_convert_fusion) | data formatting | bytes 4587520 | tf_op jit(solution)/shard_map/reshape | solution.py:45
  22.2 3.7 %maximum_bitcast_fusion = bf16[32,4,5,3584]{3,1,2,0:T(4,128)(2,1)S(1)} fusion(bf16[32,5,4,1792]{3,2,1,0:T(4,128)(2,1)S(1)} %reshape.40, bf16[32,5,4,1792]{3,2,1,0:T(4,128)(2,1)} %reshape.39), kind=kLoop, calls=%fused_computation.5 | loop fusion | flops 9175040 | bytes 9175040 | tf_op jit(solution)/shard_map/transpose | solution.py:48
  27.6 98.5 %all_to_all.10 = bf16[128,5,3584]{2,1,0:T(8,128)(2,1)} all-to-all(bf16[128,5,3584]{2,1,0:T(8,128)(2,1)S(1)} %bitcast.36), channel_id=1, replica_groups=mesh['expert'=32,'dp'=4] {'expert','dp'}, dimensions={0} | all-to-all | bytes 9175040 | tf_op jit(solution)/shard_map/all_to_all | solution.py:49
  126.1 8.1 %reshape.42 = bf16[640,3584]{1,0:T(8,128)(2,1)} reshape(bf16[128,5,3584]{2,1,0:T(8,128)(2,1)} %all_to_all.10) | data formatting | bytes 9175040 | tf_op jit(solution)/shard_map/reshape | solution.py:50
  134.2 5.4 %fusion.1 = f32[640,1024]{1,0:T(8,128)S(1)} fusion(bf16[1,1024,1792]{2,1,0:T(8,128)(2,1)} %param.13, bf16[640,3584]{1,0:T(8,128)(2,1)} %reshape.42), kind=kOutput, calls=%fused_computation.10 | convolution fusion | flops 2348810240 | bytes 8585216 | tf_op jit(solution)/shard_map/dot_general | solution.py:58
  139.7 2.5 fusion.5
  142.2 2.5 fusion.9
  144.8 3.4 pad_maximum_fusion
  148.2 72.4 %reduce-scatter.2.cloned.1.call-done = f32[160,3072]{1,0:T(8,128)} async-done(((f32[640,3072]{1,0:T(8,128)}), f32[160,3072]{1,0:T(8,128)}) %reduce-scatter.2.cloned.1.call-update) | async-done | bytes 1966096 | tf_op jit(solution)/shard_map/reduce_scatter | solution.py:61
  222.6 2.4 broadcast_in_dim.28
  226.2 2.7 collective-permute-start.1
  228.9 21.1 %collective-permute-done = bf16[160,3072]{1,0:T(8,128)(2,1)S(1)} collective-permute-done((bf16[160,3072]{1,0:T(8,128)(2,1)S(1)}, bf16[160,3072]{1,0:T(8,128)(2,1)S(1)}, u32[]{:S(2)}, u32[]{:S(2)}) %collective-permute-start) | collective-permute-done | bytes 983072 | tf_op jit(solution)/shard_map/ppermute | solution.py:78
  251.1 2.6 constant_dynamic-update-slice_fusion
  253.7 19.3 %collective-permute-done.2 = bf16[160,3072]{1,0:T(8,128)(2,1)S(1)} collective-permute-done((bf16[160,3072]{1,0:T(8,128)(2,1)S(1)}, bf16[160,3072]{1,0:T(8,128)(2,1)S(1)}, u32[]{:S(2)}, u32[]{:S(2)}) %collective-permute-start.2) | collective-permute-done | bytes 983072 | tf_op jit(solution)/shard_map/ppermute | solution.py:78
  273.9 4.0 %fusion.3 = f32[640,1792]{1,0:T(8,128)S(1)} fusion(bf16[1,1792,1024]{2,1,0:T(8,128)(2,1)S(1)} %copy-done.5, bf16[640,3072]{1,0:T(8,128)(2,1)} %constant_dynamic-update-slice_fusion.3), kind=kOutput, calls=%fused_computation.12 | convolution fusion | flops 2348810240 | bytes 9568256 | tf_op jit(solution)/shard_map/dot_general | solution.py:91
  278.0 3.9 %add_convert_fusion = bf16[640,1792]{1,0:T(8,128)(2,1)S(1)} fusion(f32[640,1792]{1,0:T(8,128)S(1)} %fusion.3, bf16[1,1792,1024]{2,1,0:T(8,128)(2,1)S(1)} %copy-done.7, bf16[640,3072]{1,0:T(8,128)(2,1)} %constant_dynamic-update-slice_fusion.3), kind=kOutput, calls=%fused_computation.6 | convolution fusion | flops 2351104000 | bytes 11862016 | tf_op jit(solution)/shard_map/dot_general | solution.py:89
  281.9 2.7 reshape.43
  284.6 9.3 %all-to-all-start.1 = ((bf16[128,5,1792]{2,1,0:T(8,128)(2,1)}), bf16[128,5,1792]{2,1,0:T(8,128)(2,1)}, u32[]{:S(2)}, u32[]{:S(2)}) async-start(bf16[128,5,1792]{2,1,0:T(8,128)(2,1)} %reshape.43), calls=%async_computation.2 | async-start | bytes 7340032 | tf_op jit(solution)/shard_map/all_to_all | solution.py:99
  294.0 7.1 %fusion.11 = bf16[1,1792,1024]{2,1,0:T(8,128)(2,1)} fusion(bf16[640,3584]{1,0:T(8,128)(2,1)} %reshape.42, bf16[640,3072]{1,0:T(8,128)(2,1)} %constant_dynamic-update-slice_fusion.3), kind=kOutput, calls=%fused_computation.20 | convolution fusion | flops 2350645248 | bytes 7274496 | tf_op jit(solution)/shard_map/dot_general | solution.py:17
  301.0 5.8 %fusion.12 = bf16[1,1792,1024]{2,1,0:T(8,128)(2,1)} fusion(bf16[640,3584]{1,0:T(8,128)(2,1)S(1)} %bitcast.40, bf16[640,3072]{1,0:T(8,128)(2,1)} %constant_dynamic-update-slice_fusion.3), kind=kOutput, calls=%fused_computation.21 | convolution fusion | flops 2350645248 | bytes 7274496 | tf_op jit(solution)/shard_map/dot_general | solution.py:17
  306.9 6.2 %fusion.13 = bf16[1,1024,1792]{2,1,0:T(8,128)(2,1)} fusion(bf16[640,3584]{1,0:T(8,128)(2,1)S(1)} %bitcast.40, bf16[640,3072]{1,0:T(8,128)(2,1)} %constant_dynamic-update-slice_fusion.3), kind=kOutput, calls=%fused_computation.22 | convolution fusion | flops 2350645248 | bytes 7274496 | tf_op jit(solution)/shard_map/dot_general | solution.py:17
  313.0 28.4 %all-to-all-done.1 = bf16[128,5,1792]{2,1,0:T(8,128)(2,1)} async-done(((bf16[128,5,1792]{2,1,0:T(8,128)(2,1)}), bf16[128,5,1792]{2,1,0:T(8,128)(2,1)}, u32[]{:S(2)}, u32[]{:S(2)}) %all-to-all-start.1) | async-done | bytes 2293792 | tf_op jit(solution)/shard_map/all_to_all | solution.py:99
  341.5 3.0 copy.34
  (45 shorter events, 15.2 us)
Async XLA Ops:
  7.2 2.5 copy-start
  7.2 213.5 %reduce-scatter.2.cloned.1.call-start = ((), (), s32[]{:S(2)}) async-start(), calls=%async_computation.3 | async-start | bytes 9830400 | tf_op jit(solution)/shard_map/reduce_scatter | solution.py:61
  8.2 7.2 %copy-start.3 = (bf16[16,7168]{1,0:T(8,128)(2,1)S(1)}, bf16[16,7168]{1,0:T(8,128)(2,1)}, u32[]{:S(2)}) copy-start(bf16[16,7168]{1,0:T(8,128)(2,1)} %param.7) | copy-start | bytes 688132
  134.2 5.4 %copy-start.2 = (bf16[640,3584]{1,0:T(8,128)(2,1)S(1)}, bf16[640,3584]{1,0:T(8,128)(2,1)}, u32[]{:S(2)}) copy-start(bf16[640,3584]{1,0:T(8,128)(2,1)} %reshape.42) | copy-start | bytes 13762564
  134.2 5.5 %copy-start.4 = (bf16[1,1792,1024]{2,1,0:T(8,128)(2,1)S(1)}, bf16[1,1792,1024]{2,1,0:T(8,128)(2,1)}, u32[]{:S(2)}) copy-start(bf16[1,1792,1024]{2,1,0:T(8,128)(2,1)} %param.12) | copy-start | bytes 11010052
  139.7 2.5 copy-start.6
  226.2 23.8 %collective-permute-start = (bf16[160,3072]{1,0:T(8,128)(2,1)S(1)}, bf16[160,3072]{1,0:T(8,128)(2,1)S(1)}, u32[]{:S(2)}, u32[]{:S(2)}) collective-permute-start(bf16[160,3072]{1,0:T(8,128)(2,1)S(1)} %get-tuple-element.7), channel_id=1, source_target_pairs={{0,1},{1,2},{2,3},{3,0},{4,5},{5,6},{6,7},{7,4},{8,9},{9,10},{10,1... | collective-permute-start | bytes 2949128 | tf_op jit(solution)/shard_map/ppermute | solution.py:78
  226.2 24.9 %collective-permute-start.1 = (bf16[160,3072]{1,0:T(8,128)(2,1)S(1)}, bf16[160,3072]{1,0:T(8,128)(2,1)}, u32[]{:S(2)}, u32[]{:S(2)}) collective-permute-start(bf16[160,3072]{1,0:T(8,128)(2,1)S(1)} %get-tuple-element.7), channel_id=1, source_target_pairs={{0,3},{1,0},{2,1},{3,2},{4,7},{5,4},{6,5},{7,6},{8,11},{9,8},{10,9... | collective-permute-start | bytes 2949128 | tf_op jit(solution)/shard_map/ppermute | solution.py:81
  250.0 22.9 %collective-permute-start.2 = (bf16[160,3072]{1,0:T(8,128)(2,1)S(1)}, bf16[160,3072]{1,0:T(8,128)(2,1)S(1)}, u32[]{:S(2)}, u32[]{:S(2)}) collective-permute-start(bf16[160,3072]{1,0:T(8,128)(2,1)S(1)} %collective-permute-done), channel_id=1, source_target_pairs={{0,1},{1,2},{2,3},{3,0},{4,5},{5,6},{6,7},{7,4},{8,9},{9,10},{10,1... | collective-permute-start | bytes 2949128 | tf_op jit(solution)/shard_map/ppermute | solution.py:78
  250.0 23.9 %copy-start.5 = (bf16[1,1792,1024]{2,1,0:T(8,128)(2,1)S(1)}, bf16[1,1792,1024]{2,1,0:T(8,128)(2,1)}, u32[]{:S(2)}) copy-start(bf16[1,1792,1024]{2,1,0:T(8,128)(2,1)} %param.12) | copy-start | bytes 11010052
  273.9 4.0 %copy-start.7 = (bf16[1,1792,1024]{2,1,0:T(8,128)(2,1)S(1)}, bf16[1,1792,1024]{2,1,0:T(8,128)(2,1)}, u32[]{:S(2)}) copy-start(bf16[1,1792,1024]{2,1,0:T(8,128)(2,1)} %param.11) | copy-start | bytes 11010052
  284.6 16.4 %slice-start = ((s8[4587520]{0:T(1024)(128)(4,1)}), s8[393216]{0:T(1024)(128)(4,1)S(1)}, s32[]{:S(2)}) async-start(s8[4587520]{0:T(1024)(128)(4,1)} %bitcast.39), calls=%async_computation.4 | async-start | bytes 786432
  284.6 56.9 %all-to-all-start.1 = ((bf16[128,5,1792]{2,1,0:T(8,128)(2,1)}), bf16[128,5,1792]{2,1,0:T(8,128)(2,1)}, u32[]{:S(2)}, u32[]{:S(2)}) async-start(bf16[128,5,1792]{2,1,0:T(8,128)(2,1)} %reshape.43), calls=%async_computation.2 | async-start | bytes 7340032 | tf_op jit(solution)/shard_map/all_to_all | solution.py:99
  294.0 7.1 %slice-start.1 = ((s8[4587520]{0:T(1024)(128)(4,1)}), s8[4194304]{0:T(1024)(128)(4,1)S(1)}, s32[]{:S(2)}) async-start(s8[4587520]{0:T(1024)(128)(4,1)} %bitcast.39), calls=%async_computation.5 | async-start | bytes 8388608
  341.5 4.5 %copy-start.1 = (bf16[16,7168]{1,0:T(8,128)(2,1)S(1)}, bf16[16,7168]{1,0:T(8,128)(2,1)}, u32[]{:S(2)}) copy-start(bf16[16,7168]{1,0:T(8,128)(2,1)} %param.8) | copy-start | bytes 688132
Sparse Core Ops, SparseCore 0:
  148.3 72.2 reduce-scatter.1
